TPU v7x, 512 devices: a whole 4x8x8 slice. The times are simulated.
512 devices in a mesh: section: 32 (over y, z_lo, core), tensor: 16 (over x, z_hi).
Axes of the slice: x: 4, y: 8, z: 8 (z_hi: 4, z_lo: 2; z = z_hi * 2 + z_lo), core: 2. Of those that a mesh axis runs over, the one named last changes fastest.
Arguments:
- tokens: bfloat16 [768, 8192], P('section', 'tensor'), may hold values from -6 to 6
- out_grad: bfloat16 [768, 8192], P('section', 'tensor'), may hold values from -3 to 3
- gate_weight: bfloat16 [8192, 14336], P('tensor', 'section'), may hold values from -0.0625 to 0.0625
- up_weight: bfloat16 [8192, 14336], P('tensor', 'section'), may hold values from -0.0625 to 0.0625
- down_weight: bfloat16 [14336, 8192], P('section', 'tensor'), may hold values from -0.046875 to 0.046875
Outputs:
- grad_input: bfloat16 [768, 8192], P('section', 'tensor')
- grad_gate: bfloat16 [8192, 14336], P('tensor', 'section')
- grad_up: bfloat16 [8192, 14336], P('tensor', 'section')
- grad_down: bfloat16 [14336, 8192], P('section', 'tensor')
All inputs are finite; a program needn't handle non-finite values.
Results may differ from a plain program's by a relative error of at most 0.0049.
Values may be sent and summed in bfloat16 or wider, within the bound.
No kernel may reach another device: no remote copies, remote signals or barrier semaphores. Data moves between devices by JAX's collectives and lax.ppermute only.
A program may use at most 64 MiB of HBM per device.

v0:
```python
import jax
import jax.numpy as jnp
from jax import lax
from jax.sharding import Mesh, PartitionSpec as P


def swiglu_grads(gate_value, up_value, hidden_grad):
    logistic = jax.nn.sigmoid(gate_value)
    swish = gate_value * logistic
    hidden = (swish * up_value).astype(jnp.bfloat16)
    up_delta = (hidden_grad * swish).astype(jnp.bfloat16)
    gate_delta = (hidden_grad * up_value * logistic * (1.0 + gate_value * (1.0 - logistic))).astype(
        jnp.bfloat16
    )
    return (hidden, gate_delta, up_delta)


SEC = ("y", "zl", "c")
TEN = ("x", "zh")


def scatter_sum(v, axis_name, n, dim):
    shape = v.shape
    v = v.reshape(shape[:dim] + (n, shape[dim] // n) + shape[dim + 1 :])
    v = lax.all_to_all(v, axis_name, dim, dim, tiled=True)
    return v.sum(dim)


def local(tokens, out_grad, gate_weight, up_weight, down_weight, nx, nzh, nsec):
    contract_last = (((1,), (1,)), ((), ()))
    contract_first = (((0,), (0,)), ((), ()))
    all_tokens, all_grads = (
        lax.all_gather(tokens, SEC, axis=0, tiled=True),
        lax.all_gather(out_grad, SEC, axis=0, tiled=True),
    )
    gate_part = jnp.dot(all_tokens, gate_weight, preferred_element_type=jnp.float32)
    up_part = jnp.dot(all_tokens, up_weight, preferred_element_type=jnp.float32)
    hidden_part = lax.dot_general(
        all_grads, down_weight, contract_last, preferred_element_type=jnp.float32
    )
    parts = jnp.stack([gate_part, up_part, hidden_part])
    parts = scatter_sum(parts, "x", nx, 1)
    parts = scatter_sum(parts, "zh", nzh, 1)
    hidden, gate_delta, up_delta = swiglu_grads(parts[0], parts[1], parts[2])
    deltas = lax.all_gather(jnp.stack([hidden, gate_delta, up_delta]), TEN, axis=1, tiled=True)
    hidden, gate_delta, up_delta = (deltas[0], deltas[1], deltas[2])
    grad_down = lax.dot_general(
        hidden, all_grads, contract_first, preferred_element_type=jnp.float32
    ).astype(jnp.bfloat16)
    grad_gate = lax.dot_general(
        all_tokens, gate_delta, contract_first, preferred_element_type=jnp.float32
    ).astype(jnp.bfloat16)
    grad_up = lax.dot_general(
        all_tokens, up_delta, contract_first, preferred_element_type=jnp.float32
    ).astype(jnp.bfloat16)
    result = lax.dot_general(
        gate_delta, gate_weight, contract_last, preferred_element_type=jnp.float32
    ) + lax.dot_general(up_delta, up_weight, contract_last, preferred_element_type=jnp.float32)
    grad_input = scatter_sum(result, SEC, nsec, 0).astype(jnp.bfloat16)
    return (grad_input, grad_gate, grad_up, grad_down)


def solution(mesh):
    nsec, nten = (mesh.shape["section"], mesh.shape["tensor"])
    nzh = 4
    nx = nten // nzh
    fine = Mesh(mesh.devices.reshape(nsec // 4, 2, 2, nx, nzh), ("y", "zl", "c", "x", "zh"))
    act = P(SEC, TEN)
    wt = P(TEN, SEC)

    def body(*args):
        return local(*args, nx=nx, nzh=nzh, nsec=nsec)

    return jax.shard_map(
        body,
        mesh=fine,
        in_specs=(act, act, wt, wt, act),
        out_specs=(act, wt, wt, act),
        check_vma=False,
    )
```

profile of v0, /device:TPU:1, one launch (start us, length us, event | category | flops | bytes accessed | tf_op | source)
XLA Modules:
  0.0 305.4 jit_solution(14879705945797379860)
XLA Ops:
  7.2 0.0 copy-start
  7.2 0.0 all-gather.2.cloned.1.call-start
  7.2 39.7 %all_gather.9 = bf16[768,512]{1,0:T(8,128)(2,1)S(1)} all-gather(bf16[24,512]{1,0:T(8,128)(2,1)} %param.5), channel_id=1, replica_groups=mesh['y'=8,'zl'=2,'c'=2,'x'=4,'zh'=4] {'y','zl','c'}, dimensions={0}, use_global_device_ids=true | all-gather | bytes 811008 | tf_op jit(solution)/shard_map/all_gather | solution.py:33
  46.9 34.7 %all_gather.10 = bf16[768,512]{1,0:T(8,128)(2,1)S(1)} all-gather(bf16[24,512]{1,0:T(8,128)(2,1)} %param.6), channel_id=1, replica_groups=mesh['y'=8,'zl'=2,'c'=2,'x'=4,'zh'=4] {'y','zl','c'}, dimensions={0}, use_global_device_ids=true | all-gather | bytes 811008 | tf_op jit(solution)/shard_map/all_gather | solution.py:34
  81.6 0.0 copy-start.1
  81.6 0.0 copy-start.4
  81.6 1.9 fusion.5
  83.5 0.0 copy-done
  83.5 0.6 fusion.4
  84.1 0.0 copy-done.1
  84.1 0.0 copy-done.4
  84.1 0.6 fusion.6
  84.7 0.5 pad_maximum_fusion
  85.3 0.5 copy.19
  85.8 57.6 %all_to_all.15 = f32[3,4,192,448]{3,2,0,1:T(8,128)} all-to-all(f32[3,4,192,448]{3,2,0,1:T(8,128)S(1)} %copy.19), channel_id=1, replica_groups=mesh['y'=8,'zl'=2,'c'=2,'x'=4,'zh'=4] {'x'}, dimensions={1} | all-to-all | bytes 8257536 | tf_op jit(solution)/shard_map/all_to_all | solution.py:25
  143.4 3.1 %reduce_sum.27 = f32[3,192,448]{2,1,0:T(8,128)S(1)} reduce(f32[3,4,192,448]{3,2,0,1:T(8,128)} %all_to_all.15, f32[]{:T(128)} %constant.0.clone.1), dimensions={1}, to_apply=%region_0.0 | reduce | flops 774144 | bytes 5160964 | tf_op jit(solution)/shard_map/reduce_sum | solution.py:26
  146.4 0.1 copy.20
  146.6 30.6 %all_to_all.16 = f32[3,4,48,448]{3,2,0,1:T(8,128)S(1)} all-to-all(f32[3,4,48,448]{3,2,0,1:T(8,128)S(1)} %copy.20), channel_id=1, replica_groups=mesh['y'=8,'zl'=2,'c'=2,'x'=4,'zh'=4] {'zh'}, dimensions={1} | all-to-all | bytes 2064384 | tf_op jit(solution)/shard_map/all_to_all | solution.py:25
  177.2 0.0 copy-start.2
  177.2 0.1 reduce_sum.28
  177.3 0.1 multiply_convert_fusion.2
  177.4 0.7 pad_maximum_fusion.1
  178.1 0.0 all-gather.2.cloned.1.call-update
  178.1 67.0 %all-gather.2.cloned.1.call-done = bf16[3,768,448]{2,1,0:T(8,128)(2,1)} async-done(((bf16[3,48,448]{2,1,0:T(8,128)(2,1)}), bf16[3,768,448]{2,1,0:T(8,128)(2,1)}) %all-gather.2.cloned.1.call-update) | async-done | bytes 2064400 | tf_op jit(solution)/shard_map/all_gather | solution.py:45
  245.1 1.7 fusion.2
  246.8 0.0 copy-done.2
  246.8 2.8 convolution_add_fusion
  249.6 9.0 %all-to-all-start.2 = ((f32[32,24,512]{2,1,0:T(8,128)}), f32[32,24,512]{2,1,0:T(8,128)S(1)}, u32[]{:S(2)}, u32[]{:S(2)}) async-start(f32[32,24,512]{2,1,0:T(8,128)} %bitcast.31), calls=%async_computation.2 | async-start | bytes 3145728 | tf_op jit(solution)/shard_map/all_to_all | solution.py:25
  258.7 0.0 copy-start.3
  258.7 2.8 convolution_convert_fusion
  261.5 0.0 copy-done.3
  261.5 1.3 fusion.1
  262.8 1.3 fusion
  264.2 33.7 %all-to-all-done.2 = f32[32,24,512]{2,1,0:T(8,128)S(1)} async-done(((f32[32,24,512]{2,1,0:T(8,128)}), f32[32,24,512]{2,1,0:T(8,128)S(1)}, u32[]{:S(2)}, u32[]{:S(2)}) %all-to-all-start.2) | async-done | bytes 1572896 | tf_op jit(solution)/shard_map/all_to_all | solution.py:25
  297.9 0.7 reduce_sum.29
Async XLA Ops:
  7.2 76.3 %copy-start = (bf16[512,448]{0,1:T(8,128)(2,1)S(1)}, bf16[512,448]{0,1:T(8,128)(2,1)}, u32[]{:S(2)}) copy-start(bf16[512,448]{0,1:T(8,128)(2,1)} %param.7) | copy-start | bytes 1376260
  7.2 237.9 %all-gather.2.cloned.1.call-start = ((), (), s32[]{:S(2)}) async-start(), calls=%async_computation.3 | async-start | bytes 2506752 | tf_op jit(solution)/shard_map/all_gather | solution.py:45
  81.6 2.5 copy-start.1
  81.6 2.5 copy-start.4
  177.2 69.6 %copy-start.2 = (bf16[512,448]{0,1:T(8,128)(2,1)S(1)}, bf16[512,448]{0,1:T(8,128)(2,1)}, u32[]{:S(2)}) copy-start(bf16[512,448]{0,1:T(8,128)(2,1)} %param.8) | copy-start | bytes 1376260
  249.6 48.2 %all-to-all-start.2 = ((f32[32,24,512]{2,1,0:T(8,128)}), f32[32,24,512]{2,1,0:T(8,128)S(1)}, u32[]{:S(2)}, u32[]{:S(2)}) async-start(f32[32,24,512]{2,1,0:T(8,128)} %bitcast.31), calls=%async_computation.2 | async-start | bytes 3145728 | tf_op jit(solution)/shard_map/all_to_all | solution.py:25
  258.7 2.9 copy-start.3
Sparse Core Ops, SparseCore 0:
  178.2 66.8 all-gather.1
where the time goes:
time: 306 us; the launch traced here: 305 us
  blocking collectives  163 us (53%)
  waiting for transfers between devices  101 us (33%)
  between operations  14.1 us (5%)
  matrix products  13.1 us (4%)
  starting transfers between devices  9.06 us (3%)
  other arithmetic  5.16 us (2%)
    all_to_all x2, blocking collectives, scatter_sum(): v = lax.all_to_all(v, axis_name, dim, dim, tiled=True)  88.2 us
    all_gather x1, waiting for transfers between devices, local(): lax.all_gather(jnp.stack([hidden, gate_delta, up_delta]), TEN, axis=1, ti...  67 us
    all_gather x1, blocking collectives, local(): lax.all_gather(tokens, SEC, axis=0, tiled=True)  39.7 us
    all_gather x1, blocking collectives, local(): lax.all_gather(out_grad, SEC, axis=0, tiled=True)  34.7 us
    all_to_all x1, waiting for transfers between devices, scatter_sum(): v = lax.all_to_all(v, axis_name, dim, dim, tiled=True)  33.7 us
    all_to_all x1, starting transfers between devices, scatter_sum(): v = lax.all_to_all(v, axis_name, dim, dim, tiled=True)  9.03 us
  transfers between devices with their start and end apart: 2, of which 2 were waited for; matrix products, arithmetic and copies ran while one was open for 2% of the time, Pallas kernels for 0%

commit v1 on v0

--- a/solution.py
+++ b/solution.py
@@ -31,7 +31,9 @@
     contract_first = (((0,), (0,)), ((), ()))
     all_tokens, all_grads = (
         lax.all_gather(tokens, SEC, axis=0, tiled=True),
-        lax.all_gather(out_grad, SEC, axis=0, tiled=True),
+        jnp.concatenate(
+            lax.all_to_all(jnp.stack([out_grad] * lax.axis_size(SEC)), SEC, 0, 0), axis=0
+        ),
     )
     gate_part = jnp.dot(all_tokens, gate_weight, preferred_element_type=jnp.float32)
     up_part = jnp.dot(all_tokens, up_weight, preferred_element_type=jnp.float32)

time: 306 us -> 297 us (0.971)
  blocking collectives: 163 us -> 137 us
  starting transfers between devices: 9.06 us -> 20.2 us
    all_gather x1 -> x0, blocking collectives: 34.7 us -> none  [local(): lax.all_gather(out_grad, SEC, axis=0, tiled=True)]
    all_to_all x0 -> x1, starting transfers between devices: none -> 11.1 us  [local(): lax.all_to_all(jnp.stack([out_grad] * lax.axis_size(SEC)), SEC, 0, 0)]
    all_gather x1, blocking collectives: 39.7 us -> 47.7 us  [local(): lax.all_gather(tokens, SEC, axis=0, tiled=True)]
  transfers between devices with their start and end apart: 2 -> 3, of which waited for: 2 -> 2; matrix products, arithmetic and copies ran while one was open for 2% -> 3% of each run, Pallas kernels for 0% -> 0%
where the time goes in v1:
time: 297 us
  blocking collectives  137 us (46%)
  waiting for transfers between devices  102 us (34%)
  starting transfers between devices  20.2 us (7%)
  matrix products  15.2 us (5%)
  between operations  14.2 us (5%)
  other arithmetic  5.31 us (2%)
    all_to_all x2, blocking collectives, scatter_sum(): v = lax.all_to_all(v, axis_name, dim, dim, tiled=True)  89.6 us
    all_gather x1, waiting for transfers between devices, local(): lax.all_gather(jnp.stack([hidden, gate_delta, up_delta]), TEN, axis=1, ti...  69.5 us
    all_gather x1, blocking collectives, local(): lax.all_gather(tokens, SEC, axis=0, tiled=True)  47.7 us
    all_to_all x1, waiting for transfers between devices, scatter_sum(): v = lax.all_to_all(v, axis_name, dim, dim, tiled=True)  32.8 us
    all_to_all x1, starting transfers between devices, local(): lax.all_to_all(jnp.stack([out_grad] * lax.axis_size(SEC)), SEC, 0, 0)  11.1 us
    all_to_all x1, starting transfers between devices, scatter_sum(): v = lax.all_to_all(v, axis_name, dim, dim, tiled=True)  9.03 us
  transfers between devices with their start and end apart: 3, of which 2 were waited for; matrix products, arithmetic and copies ran while one was open for 3% of the time, Pallas kernels for 0%

profile of v1, /device:TPU:1, one launch (start us, length us, event | category | flops | bytes accessed | tf_op | source)
XLA Modules:
  0.0 296.8 jit_solution(13251399545818002337)
XLA Ops:
  7.2 0.0 copy-start
  7.2 0.0 copy-start.4
  7.2 0.0 copy-start.2
  7.2 1.8 stack.12
  9.0 11.1 %all-to-all-start = ((bf16[32,24,512]{2,1,0:T(8,128)(2,1)}), bf16[32,24,512]{2,1,0:T(8,128)(2,1)}, u32[]{:S(2)}, u32[]{:S(2)}) async-start(bf16[32,24,512]{2,1,0:T(8,128)(2,1)} %stack.12), calls=%async_computation | async-start | bytes 1572864 | tf_op jit(solution)/shard_map/all_to_all | solution.py:35
  20.1 0.0 all-gather.2.cloned.1.call-start
  20.1 0.0 copy-done.4
  20.1 47.7 %all_gather.6 = bf16[768,512]{1,0:T(8,128)(2,1)S(1)} all-gather(bf16[24,512]{1,0:T(8,128)(2,1)S(1)} %copy-done.4), channel_id=1, replica_groups=mesh['y'=8,'zl'=2,'c'=2,'x'=4,'zh'=4] {'y','zl','c'}, dimensions={0}, use_global_device_ids=true | all-gather | bytes 811008 | tf_op jit(solution)/shard_map/all_gather | solution.py:33
  67.8 0.0 copy-done.2
  67.8 0.6 fusion.6
  68.4 0.0 copy-done
  68.4 1.8 fusion.5
  70.2 0.0 all-to-all-done
  70.2 0.0 copy-start.1
  70.2 2.0 convolution_bitcast_fusion
  72.1 0.0 copy-done.1
  72.1 0.7 pad_maximum_fusion
  72.8 0.5 copy.18
  73.3 57.6 %all_to_all.20 = f32[3,4,192,448]{3,2,0,1:T(8,128)} all-to-all(f32[3,4,192,448]{3,2,0,1:T(8,128)S(1)} %copy.18), channel_id=1, replica_groups=mesh['y'=8,'zl'=2,'c'=2,'x'=4,'zh'=4] {'x'}, dimensions={1} | all-to-all | bytes 8257536 | tf_op jit(solution)/shard_map/all_to_all | solution.py:25
  130.9 3.1 %reduce_sum.27 = f32[3,192,448]{2,1,0:T(8,128)S(1)} reduce(f32[3,4,192,448]{3,2,0,1:T(8,128)} %all_to_all.20, f32[]{:T(128)} %constant.0.clone.1), dimensions={1}, to_apply=%region_0.0 | reduce | flops 774144 | bytes 5160964 | tf_op jit(solution)/shard_map/reduce_sum | solution.py:26
  134.0 0.1 copy.19
  134.1 31.9 %all_to_all.21 = f32[3,4,48,448]{3,2,0,1:T(8,128)S(1)} all-to-all(f32[3,4,48,448]{3,2,0,1:T(8,128)S(1)} %copy.19), channel_id=1, replica_groups=mesh['y'=8,'zl'=2,'c'=2,'x'=4,'zh'=4] {'zh'}, dimensions={1} | all-to-all | bytes 2064384 | tf_op jit(solution)/shard_map/all_to_all | solution.py:25
  166.1 0.1 reduce_sum.28
  166.2 0.1 multiply_convert_fusion.2
  166.3 0.7 pad_maximum_fusion.1
  167.0 0.0 all-gather.2.cloned.1.call-update
  167.0 69.5 %all-gather.2.cloned.1.call-done = bf16[3,768,448]{2,1,0:T(8,128)(2,1)} async-done(((bf16[3,48,448]{2,1,0:T(8,128)(2,1)}), bf16[3,768,448]{2,1,0:T(8,128)(2,1)}) %all-gather.2.cloned.1.call-update) | async-done | bytes 2064400 | tf_op jit(solution)/shard_map/all_gather | solution.py:47
  236.5 1.7 fusion.2
  238.2 2.8 convolution_add_fusion
  241.1 9.0 %all-to-all-start.3 = ((f32[32,24,512]{2,1,0:T(8,128)}), f32[32,24,512]{2,1,0:T(8,128)S(1)}, u32[]{:S(2)}, u32[]{:S(2)}) async-start(f32[32,24,512]{2,1,0:T(8,128)} %bitcast.36), calls=%async_computation.3 | async-start | bytes 3145728 | tf_op jit(solution)/shard_map/all_to_all | solution.py:25
  250.1 0.0 copy-start.3
  250.1 2.6 fusion.1
  252.7 0.0 copy-done.3
  252.7 1.3 fusion
  254.0 2.4 convolution_convert_fusion
  256.5 32.8 %all-to-all-done.3 = f32[32,24,512]{2,1,0:T(8,128)S(1)} async-done(((f32[32,24,512]{2,1,0:T(8,128)}), f32[32,24,512]{2,1,0:T(8,128)S(1)}, u32[]{:S(2)}, u32[]{:S(2)}) %all-to-all-start.3) | async-done | bytes 1572896 | tf_op jit(solution)/shard_map/all_to_all | solution.py:25
  289.3 0.7 reduce_sum.29
Async XLA Ops:
  7.2 61.2 %copy-start = (bf16[512,448]{0,1:T(8,128)(2,1)S(1)}, bf16[512,448]{0,1:T(8,128)(2,1)}, u32[]{:S(2)}) copy-start(bf16[512,448]{0,1:T(8,128)(2,1)} %param.7) | copy-start | bytes 1376260
  7.2 12.9 %copy-start.4 = (bf16[24,512]{1,0:T(8,128)(2,1)S(1)}, bf16[24,512]{1,0:T(8,128)(2,1)}, u32[]{:S(2)}) copy-start(bf16[24,512]{1,0:T(8,128)(2,1)} %param.5) | copy-start | bytes 73732
  7.2 60.6 %copy-start.2 = (bf16[512,448]{0,1:T(8,128)(2,1)S(1)}, bf16[512,448]{0,1:T(8,128)(2,1)}, u32[]{:S(2)}) copy-start(bf16[512,448]{0,1:T(8,128)(2,1)} %param.8) | copy-start | bytes 1376260
  9.0 61.2 %all-to-all-start = ((bf16[32,24,512]{2,1,0:T(8,128)(2,1)}), bf16[32,24,512]{2,1,0:T(8,128)(2,1)}, u32[]{:S(2)}, u32[]{:S(2)}) async-start(bf16[32,24,512]{2,1,0:T(8,128)(2,1)} %stack.12), calls=%async_computation | async-start | bytes 1572864 | tf_op jit(solution)/shard_map/all_to_all | solution.py:35
  20.1 216.5 %all-gather.2.cloned.1.call-start = ((), (), s32[]{:S(2)}) async-start(), calls=%async_computation.4 | async-start | bytes 2506752 | tf_op jit(solution)/shard_map/all_gather | solution.py:47
  70.2 2.0 copy-start.1
  241.1 48.2 %all-to-all-start.3 = ((f32[32,24,512]{2,1,0:T(8,128)}), f32[32,24,512]{2,1,0:T(8,128)S(1)}, u32[]{:S(2)}, u32[]{:S(2)}) async-start(f32[32,24,512]{2,1,0:T(8,128)} %bitcast.36), calls=%async_computation.3 | async-start | bytes 3145728 | tf_op jit(solution)/shard_map/all_to_all | solution.py:25
  250.1 2.6 copy-start.3
Sparse Core Ops, SparseCore 0:
  167.1 69.3 all-gather.1
